TPU v7x, 256 devices: a whole 4x4x8 slice. The times are simulated.
256 devices in a mesh: gx: 32 (over x, z), gy: 8 (over y, core).
Axes of the slice: x: 4, y: 4, z: 8, core: 2. Of those that a mesh axis runs over, the one named last changes fastest.
Arguments:
- field: bfloat16 [3, 1, 48, 256, 1024], P(None, None, None, 'gx', 'gy'), may hold values from -6 to 6
- weight_x: bfloat16 [15, 48, 48], replicated, may hold values from -0.21875 to 0.21875
- weight_y: bfloat16 [15, 48, 48], replicated, may hold values from -0.21875 to 0.21875
- cotangent: bfloat16 [3, 1, 48, 256, 1024], P(None, None, None, 'gx', 'gy'), may hold values from -6 to 6
Outputs:
- output: bfloat16 [3, 1, 48, 256, 1024], P(None, None, None, 'gx', 'gy')
- field_grad: bfloat16 [3, 1, 48, 256, 1024], P(None, None, None, 'gx', 'gy')
- wx_grad: float32 [15, 48, 48], replicated
- wy_grad: float32 [15, 48, 48], replicated
All inputs are finite; a program needn't handle non-finite values.
Results may differ from a plain program's by a relative error of at most 0.0054.
Values may be sent and summed in bfloat16 or wider, within the bound.
No kernel may reach another device: no remote copies, remote signals or barrier semaphores. Data moves between devices by JAX's collectives and lax.ppermute only.
A program may use at most 64 MiB of HBM per device.

v0:
```python
import jax
import jax.numpy as jnp
from jax import lax
from jax.sharding import PartitionSpec as P


def with_halo(cells, sides, width):
    for axis, dim in sides:
        count = lax.axis_size(axis)
        ends = count - 1
        head = lax.slice_in_dim(cells, 0, width, axis=dim)
        tail = lax.slice_in_dim(cells, cells.shape[dim] - width, cells.shape[dim], axis=dim)
        cells = jnp.concatenate(
            [
                lax.ppermute(tail, axis, [(i, (i + 1) % count) for i in range(ends)]),
                cells,
                lax.ppermute(head, axis, [((i + 1) % count, i) for i in range(ends)]),
            ],
            axis=dim,
        )
    return cells


def conv_padded(padded, weight, dim):
    taps = weight.shape[0]
    length = padded.shape[dim] - taps + 1
    total = None
    for tap in range(taps):
        piece = lax.slice_in_dim(padded, tap, tap + length, axis=dim)
        term = jnp.einsum("bzcxy,co->bzoxy", piece, weight[tap], preferred_element_type=jnp.float32)
        total = term if total is None else total + term
    return total


def flipped(weight):
    return jnp.transpose(jnp.flip(weight, 0), (0, 2, 1))


def tap_products(padded, grads, taps, dim):
    length = grads.shape[dim]
    terms = []
    for tap in range(taps):
        piece = lax.slice_in_dim(padded, tap, tap + length, axis=dim)
        terms.append(
            jnp.einsum("bzcxy,bzoxy->co", piece, grads, preferred_element_type=jnp.float32)
        )
    return jnp.stack(terms)


def activate(pre):
    return jax.nn.gelu(pre.astype(jnp.float32)).astype(jnp.bfloat16)


def y_reach(values, half):
    return with_halo(values, (("gy", 4),), half)


def per_device(field, weight_x, weight_y, cotangent):
    taps = weight_x.shape[0]
    half = (taps - 1) // 2
    lines = lax.all_to_all(field, "gx", split_axis=4, concat_axis=3, tiled=True)
    lines_pad = jnp.pad(lines, ((0, 0), (0, 0), (0, 0), (half, half), (0, 0)))
    pre_lines = lax.optimization_barrier(conv_padded(lines_pad, weight_x, 3).astype(jnp.bfloat16))
    act_lines = activate(pre_lines)
    act, pre = (
        lax.all_to_all(act_lines, "gx", split_axis=3, concat_axis=4, tiled=True),
        lax.all_to_all(pre_lines, "gx", split_axis=3, concat_axis=4, tiled=True),
    )
    act_pad = y_reach(act, half)
    output = (field.astype(jnp.float32) + conv_padded(act_pad, weight_y, 4)).astype(jnp.bfloat16)
    grad_pad = y_reach(cotangent, half)
    act_grad = conv_padded(grad_pad, flipped(weight_y), 4)
    _, pull = jax.vjp(jax.nn.gelu, pre.astype(jnp.float32))
    pre_grad = pull(act_grad)[0].astype(jnp.bfloat16)
    wy_term = tap_products(act_pad, cotangent, taps, 4)
    paired = with_halo(jnp.stack((field, pre_grad)), (("gx", 4),), half)
    field_pad = paired[0]
    grad_xpad = paired[1]
    field_grad = (
        cotangent.astype(jnp.float32) + conv_padded(grad_xpad, flipped(weight_x), 3)
    ).astype(jnp.bfloat16)
    wx_term = tap_products(field_pad, pre_grad, taps, 3)
    wx_sum, wy_sum = lax.psum((wx_term, wy_term), ("gx", "gy"))
    count = (
        field.shape[0]
        * field.shape[1]
        * field.shape[3]
        * field.shape[4]
        * lax.axis_size("gx")
        * lax.axis_size("gy")
    )
    factor = 1.0 / jnp.sqrt(jnp.float32(count))
    return (output, field_grad, wx_sum * factor, wy_sum * factor)


def solution(mesh):
    in_specs = (P(None, None, None, "gx", "gy"), P(), P(), P(None, None, None, "gx", "gy"))
    out_specs = (P(None, None, None, "gx", "gy"), P(None, None, None, "gx", "gy"), P(), P())
    return jax.shard_map(
        per_device, mesh=mesh, in_specs=in_specs, out_specs=out_specs, check_vma=False
    )
```

profile of v0, /device:TPU:8, one launch (start us, length us, event | category | flops | bytes accessed | tf_op | source)
XLA Modules:
  0.0 378.1 jit_solution(10416243189057325038)
XLA Ops:
  7.2 1.6 copy.144
  8.8 1.7 reshape.644
  10.5 11.3 %all-to-all-start = ((bf16[32,2,2304]{2,1,0:T(2,128)(2,1)}), bf16[32,2,2304]{2,1,0:T(2,128)(2,1)S(1)}, u32[]{:S(2)}, u32[]{:S(2)}) async-start(bf16[32,2,2304]{2,1,0:T(2,128)(2,1)} %reshape.644), calls=%async_computation | async-start | bytes 589824 | tf_op jit(solution)/shard_map/all_to_all | solution.py:61
  22.1 1.9 collective-permute-start.3
  24.0 2.4 collective-permute-start.2
  28.1 3.9 %collective-permute-done.2 = bf16[3,1,48,8,7]{4,2,3,0,1:T(8,128)(2,1)S(1)} collective-permute-done((bf16[3,1,48,8,7]{4,2,3,0,1:T(8,128)(2,1)S(1)}, bf16[3,1,48,8,7]{4,2,3,0,1:T(8,128)(2,1)S(1)}, u32[]{:S(2)}, u32[]{:S(2)}) %collective-permute-start.2) | collective-permute-done | bytes 16160 | tf_op jit(solution)/shard_map/ppermute | solution.py:15
  35.1 1.1 fusion.6
  43.2 1.7 reshape.646
  44.9 10.0 %all-to-all-start.1 = ((bf16[32,2,2304]{2,1,0:T(2,128)(2,1)}), bf16[32,2,2304]{2,1,0:T(2,128)(2,1)S(1)}, u32[]{:S(2)}, u32[]{:S(2)}) async-start(bf16[32,2,2304]{2,1,0:T(2,128)(2,1)} %reshape.646), calls=%async_computation.1 | async-start | bytes 589824 | tf_op jit(solution)/shard_map/all_to_all | solution.py:66
  54.9 1.0 fusion.5
  58.5 1.7 reshape.648
  60.2 6.9 %all-to-all-done.1 = bf16[32,2,2304]{2,1,0:T(2,128)(2,1)S(1)} async-done(((bf16[32,2,2304]{2,1,0:T(2,128)(2,1)}), bf16[32,2,2304]{2,1,0:T(2,128)(2,1)S(1)}, u32[]{:S(2)}, u32[]{:S(2)}) %all-to-all-start.1) | async-done | bytes 294944 | tf_op jit(solution)/shard_map/all_to_all | solution.py:66
  67.1 4.7 %all-to-all-start.2 = ((bf16[32,2,2304]{2,1,0:T(2,128)(2,1)}), bf16[32,2,2304]{2,1,0:T(2,128)(2,1)S(1)}, u32[]{:S(2)}, u32[]{:S(2)}) async-start(bf16[32,2,2304]{2,1,0:T(2,128)(2,1)} %reshape.648), calls=%async_computation.2 | async-start | bytes 589824 | tf_op jit(solution)/shard_map/all_to_all | solution.py:67
  71.9 1.9 fusion.2
  76.7 1.9 collective-permute-start.1
  78.6 2.4 collective-permute-start
  81.0 1.1 fusion.178
  82.1 1.3 all-to-all-done.2
  84.6 1.3 copy.202
  85.9 1.9 fusion.65
  87.9 3.8 %collective-permute-start.4 = (bf16[2,3,1,48,7,128]{5,3,4,1,2,0:T(8,128)(2,1)S(1)}, bf16[2,3,1,48,7,128]{5,3,4,1,2,0:T(8,128)(2,1)S(1)}, u32[]{:S(2)}, u32[]{:S(2)}) collective-permute-start(bf16[2,3,1,48,7,128]{5,3,4,1,2,0:T(8,128)(2,1)S(1)} %get-tuple-element.20), channel_id=1, source_target_pairs={{0,8},{8,16},{16,24},{24,32},{32,40},{40,48},{48,56},{56,64},{64,7... | collective-permute-start | bytes 1548296 | tf_op jit(solution)/shard_map/ppermute | solution.py:15
  91.7 1.5 collective-permute-start.5
  114.6 254.6 %all-reduce.4.cloned.1.call-done = (f32[15,48,48]{2,1,0:T(8,128)}, f32[15,48,48]{2,1,0:T(8,128)}) async-done(((f32[15,48,48]{2,1,0:T(8,128)}, f32[15,48,48]{2,1,0:T(8,128)}), (f32[15,48,48]{2,1,0:T(8,128)}, f32[15,48,48]{2,1,0:T(8,128)})) %all-reduce.4.cloned.1.call-update) | async-done | bytes 276496 | tf_op jit(solution)/shard_map/psum | solution.py:83
  369.2 2.0 broadcast_multiply_fusion
  (150 shorter events, 39.3 us)
Async XLA Ops:
  7.2 14.7 %copy-start = (bf16[3,1,48,8,128]{4,3,2,1,0:T(8,128)(2,1)S(1)}, bf16[3,1,48,8,128]{4,3,2,1,0:T(8,128)(2,1)}, u32[]{:S(2)}) copy-start(bf16[3,1,48,8,128]{4,3,2,1,0:T(8,128)(2,1)} %param.7) | copy-start | bytes 884740
  8.8 17.7 %copy-start.9 = (bf16[15,48,48]{2,1,0:T(8,128)(2,1)S(1)}, bf16[15,48,48]{2,1,0:T(8,128)(2,1)}, u32[]{:S(2)}) copy-start(bf16[15,48,48]{2,1,0:T(8,128)(2,1)} %param.6) | copy-start | bytes 207364
  10.5 25.7 %all-to-all-start = ((bf16[32,2,2304]{2,1,0:T(2,128)(2,1)}), bf16[32,2,2304]{2,1,0:T(2,128)(2,1)S(1)}, u32[]{:S(2)}, u32[]{:S(2)}) async-start(bf16[32,2,2304]{2,1,0:T(2,128)(2,1)} %reshape.644), calls=%async_computation | async-start | bytes 589824 | tf_op jit(solution)/shard_map/all_to_all | solution.py:61
  21.8 4.9 %copy-start.8 = (bf16[15,48,48]{2,1,0:T(8,128)(2,1)S(1)}, bf16[15,48,48]{2,1,0:T(8,128)(2,1)}, u32[]{:S(2)}) copy-start(bf16[15,48,48]{2,1,0:T(8,128)(2,1)} %param.5) | copy-start | bytes 207364
  21.9 5.5 %copy-start.2 = (bf16[3,1,48,8,128]{4,3,2,1,0:T(8,128)(2,1)S(1)}, bf16[3,1,48,8,128]{4,3,2,1,0:T(8,128)(2,1)}, u32[]{:S(2)}) copy-start(bf16[3,1,48,8,128]{4,3,2,1,0:T(8,128)(2,1)} %param.4) | copy-start | bytes 884740
  22.1 12.6 %collective-permute-start.3 = (bf16[3,1,48,8,7]{4,2,3,0,1:T(8,128)(2,1)S(1)}, bf16[3,1,48,8,7]{4,2,3,0,1:T(8,128)(2,1)S(1)}, u32[]{:S(2)}, u32[]{:S(2)}) collective-permute-start(bf16[3,1,48,8,7]{4,2,3,0,1:T(8,128)(2,1)S(1)} %get-tuple-element.22), channel_id=1, source_target_pairs={{1,0},{2,1},{3,2},{4,3},{5,4},{6,5},{7,6},{9,8},{10,9},{11,10},{12... | collective-permute-start | bytes 48392 | tf_op jit(solution)/shard_map/ppermute | solution.py:17
  24.0 8.0 %collective-permute-start.2 = (bf16[3,1,48,8,7]{4,2,3,0,1:T(8,128)(2,1)S(1)}, bf16[3,1,48,8,7]{4,2,3,0,1:T(8,128)(2,1)S(1)}, u32[]{:S(2)}, u32[]{:S(2)}) collective-permute-start(bf16[3,1,48,8,7]{4,2,3,0,1:T(8,128)(2,1)S(1)} %get-tuple-element.23), channel_id=1, source_target_pairs={{0,1},{1,2},{2,3},{3,4},{4,5},{5,6},{6,7},{8,9},{9,10},{10,11},{11... | collective-permute-start | bytes 48392 | tf_op jit(solution)/shard_map/ppermute | solution.py:15
  26.5 8.6 %copy-start.12 = (bf16[15,48,48]{1,2,0:T(8,128)(2,1)}, bf16[15,48,48]{1,2,0:T(8,128)(2,1)S(1)}, u32[]{:S(2)}) copy-start(bf16[15,48,48]{1,2,0:T(8,128)(2,1)S(1)} %reverse_bitcast_fusion.1) | copy-start | bytes 207364
  42.4 12.5 %copy-start.5 = (f32[48,3,8,128]{3,0,2,1:T(8,128)S(1)}, f32[48,3,8,128]{3,0,2,1:T(8,128)}, u32[]{:S(2)}) copy-start(f32[48,3,8,128]{3,0,2,1:T(8,128)} %fusion.6) | copy-start | bytes 1769476
  44.9 22.2 %all-to-all-start.1 = ((bf16[32,2,2304]{2,1,0:T(2,128)(2,1)}), bf16[32,2,2304]{2,1,0:T(2,128)(2,1)S(1)}, u32[]{:S(2)}, u32[]{:S(2)}) async-start(bf16[32,2,2304]{2,1,0:T(2,128)(2,1)} %reshape.646), calls=%async_computation.1 | async-start | bytes 589824 | tf_op jit(solution)/shard_map/all_to_all | solution.py:66
  67.1 16.3 %all-to-all-start.2 = ((bf16[32,2,2304]{2,1,0:T(2,128)(2,1)}), bf16[32,2,2304]{2,1,0:T(2,128)(2,1)S(1)}, u32[]{:S(2)}, u32[]{:S(2)}) async-start(bf16[32,2,2304]{2,1,0:T(2,128)(2,1)} %reshape.648), calls=%async_computation.2 | async-start | bytes 589824 | tf_op jit(solution)/shard_map/all_to_all | solution.py:67
  71.8 297.4 %all-reduce.4.cloned.1.call-start = ((), (), s32[]{:S(2)}) async-start(), calls=%async_computation.3 | async-start | bytes 1474560 | tf_op jit(solution)/shard_map/psum | solution.py:83
  74.8 6.2 %copy-start.10 = (bf16[15,48,48]{2,1,0:T(8,128)(2,1)S(1)}, bf16[15,48,48]{2,1,0:T(8,128)(2,1)}, u32[]{:S(2)}) copy-start(bf16[15,48,48]{2,1,0:T(8,128)(2,1)} %param.6) | copy-start | bytes 207364
  75.8 8.4 %copy-start.6 = (bf16[3,48,8,128]{3,1,2,0:T(8,128)(2,1)}, bf16[3,48,8,128]{3,1,2,0:T(8,128)(2,1)S(1)}, u32[]{:S(2)}) copy-start(bf16[3,48,8,128]{3,1,2,0:T(8,128)(2,1)S(1)} %copy.179) | copy-start | bytes 884740
  76.7 19.7 %collective-permute-start.1 = (bf16[3,1,48,8,7]{4,2,3,0,1:T(8,128)(2,1)}, bf16[3,1,48,8,7]{4,2,3,0,1:T(8,128)(2,1)S(1)}, u32[]{:S(2)}, u32[]{:S(2)}) collective-permute-start(bf16[3,1,48,8,7]{4,2,3,0,1:T(8,128)(2,1)} %get-tuple-element.26), channel_id=1, source_target_pairs={{1,0},{2,1},{3,2},{4,3},{5,4},{6,5},{7,6},{9,8},{10,9},{11,10},{12... | collective-permute-start | bytes 48392 | tf_op jit(solution)/shard_map/ppermute | solution.py:17
  78.6 14.6 %collective-permute-start = (bf16[3,1,48,8,7]{4,2,3,0,1:T(8,128)(2,1)}, bf16[3,1,48,8,7]{4,2,3,0,1:T(8,128)(2,1)S(1)}, u32[]{:S(2)}, u32[]{:S(2)}) collective-permute-start(bf16[3,1,48,8,7]{4,2,3,0,1:T(8,128)(2,1)} %get-tuple-element.27), channel_id=1, source_target_pairs={{0,1},{1,2},{2,3},{3,4},{4,5},{5,6},{6,7},{8,9},{9,10},{10,11},{11... | collective-permute-start | bytes 48392 | tf_op jit(solution)/shard_map/ppermute | solution.py:15
  85.9 1.9 copy-start.1
  87.9 17.3 %collective-permute-start.4 = (bf16[2,3,1,48,7,128]{5,3,4,1,2,0:T(8,128)(2,1)S(1)}, bf16[2,3,1,48,7,128]{5,3,4,1,2,0:T(8,128)(2,1)S(1)}, u32[]{:S(2)}, u32[]{:S(2)}) collective-permute-start(bf16[2,3,1,48,7,128]{5,3,4,1,2,0:T(8,128)(2,1)S(1)} %get-tuple-element.20), channel_id=1, source_target_pairs={{0,8},{8,16},{16,24},{24,32},{32,40},{40,48},{48,56},{56,64},{64,7... | collective-permute-start | bytes 1548296 | tf_op jit(solution)/shard_map/ppermute | solution.py:15
  91.7 14.8 %collective-permute-start.5 = (bf16[2,3,1,48,7,128]{5,3,4,1,2,0:T(8,128)(2,1)S(1)}, bf16[2,3,1,48,7,128]{5,3,4,1,2,0:T(8,128)(2,1)S(1)}, u32[]{:S(2)}, u32[]{:S(2)}) collective-permute-start(bf16[2,3,1,48,7,128]{5,3,4,1,2,0:T(8,128)(2,1)S(1)} %get-tuple-element.21), channel_id=1, source_target_pairs={{8,0},{16,8},{24,16},{32,24},{40,32},{48,40},{56,48},{64,56},{72,6... | collective-permute-start | bytes 1548296 | tf_op jit(solution)/shard_map/ppermute | solution.py:17
  94.6 1.1 copy-start.7
  98.9 1.1 copy-start.4
  102.0 1.0 copy-start.3
  105.2 0.7 copy-start.13
  109.3 1.2 copy-start.11
  (1 other events, 0.7 us)
Sparse Core Ops, SparseCore 0:
  113.7 255.4 all-reduce.3
where the time goes:
time: 379 us; the launch traced here: 378 us
  waiting for transfers between devices  267 us (70%)
  starting transfers between devices  40 us (11%)
  matrix products  33.7 us (9%)
  local copies, waits for them, and re-layouts  19.4 us (5%)
  between operations  15.2 us (4%)
    psum x1, waiting for transfers between devices, per_device(): wx_sum, wy_sum = lax.psum((wx_term, wy_term), ('gx', 'gy'))  255 us
    dot_general x60, matrix products, conv_padded(): jnp.einsum('bzcxy,co->bzoxy', piece, weight[tap], preferred_element_type=...  25.2 us
    unnamed x41, local copies, waits for them, and re-layouts  12.9 us
    all_to_all x1, starting transfers between devices, per_device(): lines = lax.all_to_all(field, 'gx', split_axis=4, concat_axis=3, tiled=True)  11.3 us
    all_to_all x1, starting transfers between devices, per_device(): lax.all_to_all(act_lines, 'gx', split_axis=3, concat_axis=4, tiled=True)  9.97 us
    ppermute x3, starting transfers between devices, with_halo(): lax.ppermute(tail, axis, [(i, (i + 1) % count) for i in range(ends)])  8.62 us
    dot_general x30, matrix products, tap_products(): jnp.einsum('bzcxy,bzoxy->co', piece, grads, preferred_element_type=jnp.fl...  8.47 us
  transfers between devices with their start and end apart: 10, of which 5 were waited for; matrix products, arithmetic and copies ran while one was open for 9% of the time, Pallas kernels for 0%

commit v1 on v0

--- a/solution.py
+++ b/solution.py
@@ -80,7 +80,7 @@
         cotangent.astype(jnp.float32) + conv_padded(grad_xpad, flipped(weight_x), 3)
     ).astype(jnp.bfloat16)
     wx_term = tap_products(field_pad, pre_grad, taps, 3)
-    wx_sum, wy_sum = lax.psum((wx_term, wy_term), ("gx", "gy"))
+    wx_sum, wy_sum = lax.psum(lax.psum((wx_term, wy_term), "gx"), "gy")
     count = (
         field.shape[0]
         * field.shape[1]

time: 379 us -> 339 us (0.89)
  waiting for transfers between devices: 267 us -> 225 us
    psum x1 -> x2, waiting for transfers between devices: 255 us -> 212 us  [per_device(): wx_sum, wy_sum = lax.psum(lax.psum((wx_term, wy_term), 'gx'), 'gy')]
  transfers between devices with their start and end apart: 10 -> 11, of which waited for: 5 -> 6; matrix products, arithmetic and copies ran while one was open for 9% -> 10% of each run, Pallas kernels for 0% -> 0%
where the time goes in v1:
time: 339 us; the launch traced here: 336 us
  waiting for transfers between devices  225 us (66%)
  starting transfers between devices  40 us (12%)
  matrix products  33.7 us (10%)
  local copies, waits for them, and re-layouts  19.4 us (6%)
  between operations  15.2 us (4%)
    psum x2, waiting for transfers between devices, per_device(): wx_sum, wy_sum = lax.psum(lax.psum((wx_term, wy_term), 'gx'), 'gy')  212 us
    dot_general x60, matrix products, conv_padded(): jnp.einsum('bzcxy,co->bzoxy', piece, weight[tap], preferred_element_type=...  25.2 us
    unnamed x41, local copies, waits for them, and re-layouts  12.9 us
    all_to_all x1, starting transfers between devices, per_device(): lines = lax.all_to_all(field, 'gx', split_axis=4, concat_axis=3, tiled=True)  11.3 us
    all_to_all x1, starting transfers between devices, per_device(): lax.all_to_all(act_lines, 'gx', split_axis=3, concat_axis=4, tiled=True)  9.96 us
    ppermute x3, starting transfers between devices, with_halo(): lax.ppermute(tail, axis, [(i, (i + 1) % count) for i in range(ends)])  8.62 us
    dot_general x30, matrix products, tap_products(): jnp.einsum('bzcxy,bzoxy->co', piece, grads, preferred_element_type=jnp.fl...  8.47 us
    all_to_all x1, waiting for transfers between devices, per_device(): lax.all_to_all(act_lines, 'gx', split_axis=3, concat_axis=4, tiled=True)  6.88 us
  transfers between devices with their start and end apart: 11, of which 6 were waited for; matrix products, arithmetic and copies ran while one was open for 10% of the time, Pallas kernels for 0%

profile of v1, /device:TPU:8, one launch (start us, length us, event | category | flops | bytes accessed | tf_op | source)
XLA Modules:
  0.0 335.9 jit_solution(2623708726200113873)
XLA Ops:
  7.2 1.6 copy.144
  8.8 1.7 reshape.644
  10.5 11.3 %all-to-all-start = ((bf16[32,2,2304]{2,1,0:T(2,128)(2,1)}), bf16[32,2,2304]{2,1,0:T(2,128)(2,1)S(1)}, u32[]{:S(2)}, u32[]{:S(2)}) async-start(bf16[32,2,2304]{2,1,0:T(2,128)(2,1)} %reshape.644), calls=%async_computation | async-start | bytes 589824 | tf_op jit(solution)/shard_map/all_to_all | solution.py:61
  22.1 1.9 collective-permute-start.3
  24.0 2.4 collective-permute-start.2
  28.2 3.9 %collective-permute-done.2 = bf16[3,1,48,8,7]{4,2,3,0,1:T(8,128)(2,1)S(1)} collective-permute-done((bf16[3,1,48,8,7]{4,2,3,0,1:T(8,128)(2,1)S(1)}, bf16[3,1,48,8,7]{4,2,3,0,1:T(8,128)(2,1)S(1)}, u32[]{:S(2)}, u32[]{:S(2)}) %collective-permute-start.2) | collective-permute-done | bytes 16160 | tf_op jit(solution)/shard_map/ppermute | solution.py:15
  35.1 1.1 fusion.6
  43.2 1.7 reshape.646
  44.9 10.0 %all-to-all-start.1 = ((bf16[32,2,2304]{2,1,0:T(2,128)(2,1)}), bf16[32,2,2304]{2,1,0:T(2,128)(2,1)S(1)}, u32[]{:S(2)}, u32[]{:S(2)}) async-start(bf16[32,2,2304]{2,1,0:T(2,128)(2,1)} %reshape.646), calls=%async_computation.1 | async-start | bytes 589824 | tf_op jit(solution)/shard_map/all_to_all | solution.py:66
  58.5 1.7 reshape.648
  60.2 6.9 %all-to-all-done.1 = bf16[32,2,2304]{2,1,0:T(2,128)(2,1)S(1)} async-done(((bf16[32,2,2304]{2,1,0:T(2,128)(2,1)}), bf16[32,2,2304]{2,1,0:T(2,128)(2,1)S(1)}, u32[]{:S(2)}, u32[]{:S(2)}) %all-to-all-start.1) | async-done | bytes 294944 | tf_op jit(solution)/shard_map/all_to_all | solution.py:66
  67.1 4.7 %all-to-all-start.2 = ((bf16[32,2,2304]{2,1,0:T(2,128)(2,1)}), bf16[32,2,2304]{2,1,0:T(2,128)(2,1)S(1)}, u32[]{:S(2)}, u32[]{:S(2)}) async-start(bf16[32,2,2304]{2,1,0:T(2,128)(2,1)} %reshape.648), calls=%async_computation.2 | async-start | bytes 589824 | tf_op jit(solution)/shard_map/all_to_all | solution.py:67
  71.9 1.9 fusion.2
  76.7 1.9 collective-permute-start.1
  78.6 2.4 collective-permute-start
  81.0 1.1 fusion.178
  82.1 1.3 all-to-all-done.2
  84.6 1.3 copy.202
  85.9 1.9 fusion.65
  87.9 3.8 %collective-permute-start.4 = (bf16[2,3,1,48,7,128]{5,3,4,1,2,0:T(8,128)(2,1)S(1)}, bf16[2,3,1,48,7,128]{5,3,4,1,2,0:T(8,128)(2,1)S(1)}, u32[]{:S(2)}, u32[]{:S(2)}) collective-permute-start(bf16[2,3,1,48,7,128]{5,3,4,1,2,0:T(8,128)(2,1)S(1)} %get-tuple-element.22), channel_id=1, source_target_pairs={{0,8},{8,16},{16,24},{24,32},{32,40},{40,48},{48,56},{56,64},{64,7... | collective-permute-start | bytes 1548296 | tf_op jit(solution)/shard_map/ppermute | solution.py:15
  91.7 1.5 collective-permute-start.5
  113.7 149.4 %all-reduce.6.cloned.1.call-done = (f32[15,48,48]{2,1,0:T(8,128)}, f32[15,48,48]{2,1,0:T(8,128)}) async-done(((f32[15,48,48]{2,1,0:T(8,128)}, f32[15,48,48]{2,1,0:T(8,128)}), (f32[15,48,48]{2,1,0:T(8,128)}, f32[15,48,48]{2,1,0:T(8,128)})) %all-reduce.6.cloned.1.call-update) | async-done | bytes 276496 | tf_op jit(solution)/shard_map/psum | solution.py:83
  264.2 62.9 %all-reduce.8.cloned.1.call-done = (f32[15,48,48]{2,1,0:T(8,128)}, f32[15,48,48]{2,1,0:T(8,128)}) async-done(((f32[15,48,48]{2,1,0:T(8,128)}, f32[15,48,48]{2,1,0:T(8,128)}), (f32[15,48,48]{2,1,0:T(8,128)}, f32[15,48,48]{2,1,0:T(8,128)})) %all-reduce.8.cloned.1.call-update) | async-done | bytes 276496 | tf_op jit(solution)/shard_map/psum | solution.py:83
  327.1 2.0 broadcast_multiply_fusion
  (153 shorter events, 40.4 us)
Async XLA Ops:
  7.2 14.7 %copy-start = (bf16[3,1,48,8,128]{4,3,2,1,0:T(8,128)(2,1)S(1)}, bf16[3,1,48,8,128]{4,3,2,1,0:T(8,128)(2,1)}, u32[]{:S(2)}) copy-start(bf16[3,1,48,8,128]{4,3,2,1,0:T(8,128)(2,1)} %param.7) | copy-start | bytes 884740
  8.8 17.7 %copy-start.9 = (bf16[15,48,48]{2,1,0:T(8,128)(2,1)S(1)}, bf16[15,48,48]{2,1,0:T(8,128)(2,1)}, u32[]{:S(2)}) copy-start(bf16[15,48,48]{2,1,0:T(8,128)(2,1)} %param.6) | copy-start | bytes 207364
  10.5 25.7 %all-to-all-start = ((bf16[32,2,2304]{2,1,0:T(2,128)(2,1)}), bf16[32,2,2304]{2,1,0:T(2,128)(2,1)S(1)}, u32[]{:S(2)}, u32[]{:S(2)}) async-start(bf16[32,2,2304]{2,1,0:T(2,128)(2,1)} %reshape.644), calls=%async_computation | async-start | bytes 589824 | tf_op jit(solution)/shard_map/all_to_all | solution.py:61
  21.8 4.9 %copy-start.8 = (bf16[15,48,48]{2,1,0:T(8,128)(2,1)S(1)}, bf16[15,48,48]{2,1,0:T(8,128)(2,1)}, u32[]{:S(2)}) copy-start(bf16[15,48,48]{2,1,0:T(8,128)(2,1)} %param.5) | copy-start | bytes 207364
  21.9 5.5 %copy-start.2 = (bf16[3,1,48,8,128]{4,3,2,1,0:T(8,128)(2,1)S(1)}, bf16[3,1,48,8,128]{4,3,2,1,0:T(8,128)(2,1)}, u32[]{:S(2)}) copy-start(bf16[3,1,48,8,128]{4,3,2,1,0:T(8,128)(2,1)} %param.4) | copy-start | bytes 884740
  22.1 12.6 %collective-permute-start.3 = (bf16[3,1,48,8,7]{4,2,3,0,1:T(8,128)(2,1)S(1)}, bf16[3,1,48,8,7]{4,2,3,0,1:T(8,128)(2,1)S(1)}, u32[]{:S(2)}, u32[]{:S(2)}) collective-permute-start(bf16[3,1,48,8,7]{4,2,3,0,1:T(8,128)(2,1)S(1)} %get-tuple-element.24), channel_id=1, source_target_pairs={{1,0},{2,1},{3,2},{4,3},{5,4},{6,5},{7,6},{9,8},{10,9},{11,10},{12... | collective-permute-start | bytes 48392 | tf_op jit(solution)/shard_map/ppermute | solution.py:17
  24.0 8.0 %collective-permute-start.2 = (bf16[3,1,48,8,7]{4,2,3,0,1:T(8,128)(2,1)S(1)}, bf16[3,1,48,8,7]{4,2,3,0,1:T(8,128)(2,1)S(1)}, u32[]{:S(2)}, u32[]{:S(2)}) collective-permute-start(bf16[3,1,48,8,7]{4,2,3,0,1:T(8,128)(2,1)S(1)} %get-tuple-element.25), channel_id=1, source_target_pairs={{0,1},{1,2},{2,3},{3,4},{4,5},{5,6},{6,7},{8,9},{9,10},{10,11},{11... | collective-permute-start | bytes 48392 | tf_op jit(solution)/shard_map/ppermute | solution.py:15
  26.5 8.6 %copy-start.12 = (bf16[15,48,48]{1,2,0:T(8,128)(2,1)}, bf16[15,48,48]{1,2,0:T(8,128)(2,1)S(1)}, u32[]{:S(2)}) copy-start(bf16[15,48,48]{1,2,0:T(8,128)(2,1)S(1)} %reverse_bitcast_fusion.1) | copy-start | bytes 207364
  42.4 12.5 %copy-start.5 = (f32[48,3,8,128]{3,0,2,1:T(8,128)S(1)}, f32[48,3,8,128]{3,0,2,1:T(8,128)}, u32[]{:S(2)}) copy-start(f32[48,3,8,128]{3,0,2,1:T(8,128)} %fusion.6) | copy-start | bytes 1769476
  44.9 22.2 %all-to-all-start.1 = ((bf16[32,2,2304]{2,1,0:T(2,128)(2,1)}), bf16[32,2,2304]{2,1,0:T(2,128)(2,1)S(1)}, u32[]{:S(2)}, u32[]{:S(2)}) async-start(bf16[32,2,2304]{2,1,0:T(2,128)(2,1)} %reshape.646), calls=%async_computation.1 | async-start | bytes 589824 | tf_op jit(solution)/shard_map/all_to_all | solution.py:66
  67.1 16.3 %all-to-all-start.2 = ((bf16[32,2,2304]{2,1,0:T(2,128)(2,1)}), bf16[32,2,2304]{2,1,0:T(2,128)(2,1)S(1)}, u32[]{:S(2)}, u32[]{:S(2)}) async-start(bf16[32,2,2304]{2,1,0:T(2,128)(2,1)} %reshape.648), calls=%async_computation.2 | async-start | bytes 589824 | tf_op jit(solution)/shard_map/all_to_all | solution.py:67
  71.8 191.3 %all-reduce.6.cloned.1.call-start = ((), (), s32[]{:S(2)}) async-start(), calls=%async_computation.3 | async-start | bytes 1474560 | tf_op jit(solution)/shard_map/psum | solution.py:83
  74.8 6.2 %copy-start.10 = (bf16[15,48,48]{2,1,0:T(8,128)(2,1)S(1)}, bf16[15,48,48]{2,1,0:T(8,128)(2,1)}, u32[]{:S(2)}) copy-start(bf16[15,48,48]{2,1,0:T(8,128)(2,1)} %param.6) | copy-start | bytes 207364
  75.8 8.4 %copy-start.6 = (bf16[3,48,8,128]{3,1,2,0:T(8,128)(2,1)}, bf16[3,48,8,128]{3,1,2,0:T(8,128)(2,1)S(1)}, u32[]{:S(2)}) copy-start(bf16[3,48,8,128]{3,1,2,0:T(8,128)(2,1)S(1)} %copy.179) | copy-start | bytes 884740
  76.7 19.7 %collective-permute-start.1 = (bf16[3,1,48,8,7]{4,2,3,0,1:T(8,128)(2,1)}, bf16[3,1,48,8,7]{4,2,3,0,1:T(8,128)(2,1)S(1)}, u32[]{:S(2)}, u32[]{:S(2)}) collective-permute-start(bf16[3,1,48,8,7]{4,2,3,0,1:T(8,128)(2,1)} %get-tuple-element.28), channel_id=1, source_target_pairs={{1,0},{2,1},{3,2},{4,3},{5,4},{6,5},{7,6},{9,8},{10,9},{11,10},{12... | collective-permute-start | bytes 48392 | tf_op jit(solution)/shard_map/ppermute | solution.py:17
  78.6 14.6 %collective-permute-start = (bf16[3,1,48,8,7]{4,2,3,0,1:T(8,128)(2,1)}, bf16[3,1,48,8,7]{4,2,3,0,1:T(8,128)(2,1)S(1)}, u32[]{:S(2)}, u32[]{:S(2)}) collective-permute-start(bf16[3,1,48,8,7]{4,2,3,0,1:T(8,128)(2,1)} %get-tuple-element.29), channel_id=1, source_target_pairs={{0,1},{1,2},{2,3},{3,4},{4,5},{5,6},{6,7},{8,9},{9,10},{10,11},{11... | collective-permute-start | bytes 48392 | tf_op jit(solution)/shard_map/ppermute | solution.py:15
  85.9 1.9 copy-start.1
  87.9 17.3 %collective-permute-start.4 = (bf16[2,3,1,48,7,128]{5,3,4,1,2,0:T(8,128)(2,1)S(1)}, bf16[2,3,1,48,7,128]{5,3,4,1,2,0:T(8,128)(2,1)S(1)}, u32[]{:S(2)}, u32[]{:S(2)}) collective-permute-start(bf16[2,3,1,48,7,128]{5,3,4,1,2,0:T(8,128)(2,1)S(1)} %get-tuple-element.22), channel_id=1, source_target_pairs={{0,8},{8,16},{16,24},{24,32},{32,40},{40,48},{48,56},{56,64},{64,7... | collective-permute-start | bytes 1548296 | tf_op jit(solution)/shard_map/ppermute | solution.py:15
  91.7 14.8 %collective-permute-start.5 = (bf16[2,3,1,48,7,128]{5,3,4,1,2,0:T(8,128)(2,1)S(1)}, bf16[2,3,1,48,7,128]{5,3,4,1,2,0:T(8,128)(2,1)S(1)}, u32[]{:S(2)}, u32[]{:S(2)}) collective-permute-start(bf16[2,3,1,48,7,128]{5,3,4,1,2,0:T(8,128)(2,1)S(1)} %get-tuple-element.23), channel_id=1, source_target_pairs={{8,0},{16,8},{24,16},{32,24},{40,32},{48,40},{56,48},{64,56},{72,6... | collective-permute-start | bytes 1548296 | tf_op jit(solution)/shard_map/ppermute | solution.py:17
  94.6 1.1 copy-start.7
  98.9 1.1 copy-start.4
  102.0 1.0 copy-start.3
  109.3 1.2 copy-start.11
  113.2 213.9 %all-reduce.8.cloned.1.call-start = ((), (), s32[]{:S(2)}) async-start(), calls=%async_computation.4 | async-start | bytes 1474560 | tf_op jit(solution)/shard_map/psum | solution.py:83
  (2 other events, 1.5 us)
Sparse Core Ops, SparseCore 0:
  113.3 149.7 all-reduce.5
  265.7 61.3 all-reduce.7
